TPU v7x, 128 devices: a whole 4x4x4 slice. The times are simulated.
128 devices in a mesh: row: 8 (over y, z_hi), col: 16 (over z_lo, x, core).
Axes of the slice: x: 4, y: 4, z: 4 (z_hi: 2, z_lo: 2; z = z_hi * 2 + z_lo), core: 2. Of those that a mesh axis runs over, the one named last changes fastest.
Arguments:
- upper_stored: bfloat16 [6144, 6144], P('row', 'col'), may hold values from -6 to 6
- block_cells: int32 [96, 3], replicated, may hold values from 0 to 15
Outputs:
- purified: bfloat16 [6144, 6144], P('row', 'col')
Inputs may be any that keep to these rules, and one draw needn't show every extreme that they name: `block_cells`: integer cell coordinates of each atom block on a periodic lattice of 16 cells a side.
All inputs are finite; a program needn't handle non-finite values.
Results may differ from a plain program's by a relative error of at most 0.0067.
Values may be sent and summed in bfloat16 or wider, within the bound.
No kernel may reach another device: no remote copies, remote signals or barrier semaphores. Data moves between devices by JAX's collectives and lax.ppermute only.
A program may use at most 64 MiB of HBM per device.

v0:
```python
import math
import jax
import jax.numpy as jnp
from jax import lax
from jax.sharding import PartitionSpec as P

BLK = 64
BOX = 16
NEAR = 40
FAR = 90


def cell_mask(block_cells, row_start, row_count, col_start, col_count, bound_sq):
    row_cells = lax.dynamic_slice_in_dim(block_cells, row_start, row_count, 0)
    col_cells = lax.dynamic_slice_in_dim(block_cells, col_start, col_count, 0)
    offset_abs = jnp.abs(row_cells[:, None, :] - col_cells[None, :, :])
    wrapped = jnp.minimum(offset_abs, BOX - offset_abs)
    return jnp.sum(wrapped * wrapped, axis=2) <= bound_sq


def block_keep(matrix_tile, keep_mask):
    row_count, col_count = matrix_tile.shape
    row_blocks, col_blocks = keep_mask.shape
    shaped = matrix_tile.reshape(
        row_blocks, row_count // row_blocks, col_blocks, col_count // col_blocks
    )
    kept = jnp.where(keep_mask[:, None, :, None], shaped, jnp.zeros_like(shaped))
    return kept.reshape(row_count, col_count)


def mirror_tile(upper_stored, rows, cols):
    tile_side, half_width = upper_stored.shape
    row_id = lax.axis_index("row")
    col_id = lax.axis_index("col")
    pieces = []
    for k in range(2):
        half = (col_id + k) % 2
        piece = lax.dynamic_slice_in_dim(upper_stored, half * half_width, half_width, 0)
        pairs = []
        for a in range(rows):
            for b in range(cols):
                h = (b + k) % 2
                pairs.append((a * cols + b, b // 2 * cols + 2 * a + h))
        pieces.append(lax.ppermute(piece, ("row", "col"), pairs))
    h_own = col_id % 2
    first = jnp.where(h_own == 0, pieces[0], pieces[1])
    second = jnp.where(h_own == 0, pieces[1], pieces[0])
    return jnp.concatenate([first, second], 1).T


def per_device(upper_stored, block_cells):
    rows = lax.axis_size("row")
    cols = lax.axis_size("col")
    row_id = lax.axis_index("row")
    col_id = lax.axis_index("col")
    tile_side, half_width = upper_stored.shape
    order_total = tile_side * rows
    tile_blocks = tile_side // BLK
    half_blocks = half_width // BLK
    mirrored = mirror_tile(upper_stored, rows, cols)
    global_rows = row_id * tile_side + lax.broadcasted_iota(jnp.int32, (tile_side, half_width), 0)
    global_cols = col_id * half_width + lax.broadcasted_iota(jnp.int32, (tile_side, half_width), 1)
    symmetric = jnp.where(global_rows <= global_cols, upper_stored, mirrored)
    near_own = cell_mask(
        block_cells, row_id * tile_blocks, tile_blocks, col_id * half_blocks, half_blocks, NEAR
    )
    far_own = cell_mask(
        block_cells, row_id * tile_blocks, tile_blocks, col_id * half_blocks, half_blocks, FAR
    )
    diagonal = jnp.where(global_rows == global_cols, 0.5, 0.0).astype(jnp.float32)
    value_scale = 2.0 / math.sqrt(order_total)
    density = block_keep(diagonal + value_scale * symmetric.astype(jnp.float32), near_own).astype(
        jnp.bfloat16
    )
    row_panel = lax.all_gather(density, "col", axis=1, tiled=True)
    col_panel = lax.all_gather(density, "row", axis=0, tiled=True)
    square = block_keep(jnp.dot(row_panel, col_panel, preferred_element_type=jnp.float32), far_own)
    square_low = square.astype(jnp.bfloat16)
    low_panel = lax.all_gather(square_low, "col", axis=1, tiled=True)
    cubic = jnp.dot(low_panel, col_panel, preferred_element_type=jnp.float32)
    return block_keep(3.0 * square - 2.0 * cubic, near_own).astype(jnp.bfloat16)


def solution(mesh):
    return jax.shard_map(
        per_device,
        mesh=mesh,
        in_specs=(P("row", "col"), P()),
        out_specs=P("row", "col"),
        check_vma=False,
    )
```

profile of v0, /device:TPU:1, one launch (start us, length us, event | category | flops | bytes accessed | tf_op | source)
XLA Modules:
  0.0 260.0 jit_solution(1769030043585015134)
XLA Ops:
  6.5 0.0 copy-start
  6.5 0.0 all-gather.6.cloned.1.call-start
  6.5 1.1 constant_dynamic-slice_fusion.1
  7.7 0.2 copy.16
  7.9 1.5 collective-permute-start.1
  9.3 0.2 copy.15
  9.6 0.7 collective-permute-start
  10.3 0.0 copy-done
  10.3 0.1 constant_dynamic-slice_fusion.2
  10.3 0.1 constant_dynamic-slice_fusion.3
  10.4 0.1 fusion.4
  10.5 0.1 copy.11
  10.6 0.3 broadcast_in_dim.35
  10.9 0.0 copy-start.1
  10.9 1.4 broadcast_in_dim.36
  12.3 0.0 collective-permute-done.1
  12.3 0.0 collective-permute-done
  12.4 0.1 broadcast_select_fusion.1
  12.4 1.3 select_convert_fusion
  13.8 0.0 all-gather.6.cloned.1.call-update
  13.8 0.0 all-gather.4.cloned.1.call-start
  13.9 0.7 all-gather.4.cloned.1.call-update
  14.6 0.0 all-gather.8.cloned.1.call-start
  14.6 0.1 copy.12
  14.7 0.3 broadcast_in_dim.37
  15.0 1.4 broadcast_in_dim.38
  16.4 102.2 %all-gather.6.cloned.1.call-done = bf16[6144,384]{1,0:T(8,128)(2,1)} async-done(((bf16[768,384]{1,0:T(8,128)(2,1)}), bf16[6144,384]{1,0:T(8,128)(2,1)}) %all-gather.6.cloned.1.call-update) | async-done | bytes 4718608 | tf_op jit(solution)/shard_map/all_gather | solution.py:76
  118.6 57.4 %all-gather.4.cloned.1.call-done = bf16[768,6144]{1,0:T(8,128)(2,1)} async-done(((bf16[768,384]{1,0:T(8,128)(2,1)}), bf16[768,6144]{1,0:T(8,128)(2,1)}) %all-gather.4.cloned.1.call-update) | async-done | bytes 9437200 | tf_op jit(solution)/shard_map/all_gather | solution.py:75
  176.0 9.7 %fusion.5 = (bf16[768,384]{1,0:T(8,128)(2,1)}, f32[768,384]{1,0:T(8,128)S(1)}) fusion(pred[768,384]{1,0:T(32,128)(4,1)S(1)} %broadcast_in_dim.38, bf16[768,6144]{1,0:T(8,128)(2,1)} %all-gather.4.cloned.1.call-done, bf16[6144,384]{1,0:T(8,128)(2,1)} %all-gather.6.cloned.1.call-done), kind=kOutput, calls=%fused_computation.21 | convolution fusion | flops 3624468480 | bytes 16220160 | tf_op jit(solution)/shard_map/dot_general | solution.py:77
  185.7 0.0 all-gather.8.cloned.1.call-update
  185.7 58.0 %all-gather.8.cloned.1.call-done = bf16[768,6144]{1,0:T(8,128)(2,1)} async-done(((bf16[768,384]{1,0:T(8,128)(2,1)}), bf16[768,6144]{1,0:T(8,128)(2,1)}) %all-gather.8.cloned.1.call-update) | async-done | bytes 9437200 | tf_op jit(solution)/shard_map/all_gather | solution.py:79
  243.7 9.7 %fusion.2 = bf16[768,384]{1,0:T(8,128)(2,1)} fusion(pred[768,384]{1,0:T(32,128)(4,1)S(1)} %broadcast_in_dim.36, bf16[768,6144]{1,0:T(8,128)(2,1)} %all-gather.8.cloned.1.call-done, bf16[6144,384]{1,0:T(8,128)(2,1)} %all-gather.6.cloned.1.call-done, f32[768,384]{1,0:T(8,128)S(1)} %get-tuple-element.12), kind=kOutput, calls=%fused_computation.4 | convolution fusion | flops 3625353216 | bytes 16220160 | tf_op jit(solution)/shard_map/dot_general | solution.py:80
  (4 shorter events, 0.0 us)
Async XLA Ops:
  6.5 3.7 %copy-start = (s32[96,3]{0,1:T(4,128)S(1)}, s32[96,3]{0,1:T(4,128)}, u32[]{:S(2)}) copy-start(s32[96,3]{0,1:T(4,128)} %param.3) | copy-start | bytes 3460
  6.5 112.0 %all-gather.6.cloned.1.call-start = ((), (), s32[]{:S(2)}) async-start(), calls=%async_computation.1 | async-start | bytes 5308416 | tf_op jit(solution)/shard_map/all_gather | solution.py:76
  7.9 4.5 %collective-permute-start.1 = (bf16[384,384]{0,1:T(8,128)(2,1)S(1)}, bf16[384,384]{0,1:T(8,128)(2,1)S(1)}, u32[]{:S(2)}, u32[]{:S(2)}) collective-permute-start(bf16[384,384]{0,1:T(8,128)(2,1)S(1)} %copy.16), channel_id=1, source_target_pairs={{0,1},{1,0},{2,17},{3,16},{4,33},{5,32},{6,49},{7,48},{8,65},{9,64... | collective-permute-start | bytes 884744 | tf_op jit(solution)/shard_map/ppermute | solution.py:44
  9.6 2.8 %collective-permute-start = (bf16[384,384]{0,1:T(8,128)(2,1)S(1)}, bf16[384,384]{0,1:T(8,128)(2,1)S(1)}, u32[]{:S(2)}, u32[]{:S(2)}) collective-permute-start(bf16[384,384]{0,1:T(8,128)(2,1)S(1)} %copy.15), channel_id=1, source_target_pairs={{0,0},{1,1},{2,16},{3,17},{4,32},{5,33},{6,48},{7,49},{8,64},{9,65... | collective-permute-start | bytes 884744 | tf_op jit(solution)/shard_map/ppermute | solution.py:44
  10.9 1.5 copy-start.1
  13.8 162.2 %all-gather.4.cloned.1.call-start = ((), (), s32[]{:S(2)}) async-start(), calls=%async_computation | async-start | bytes 10027008 | tf_op jit(solution)/shard_map/all_gather | solution.py:75
  14.6 229.1 %all-gather.8.cloned.1.call-start = ((), (), s32[]{:S(2)}) async-start(), calls=%async_computation.2 | async-start | bytes 10027008 | tf_op jit(solution)/shard_map/all_gather | solution.py:79
Sparse Core Ops, SparseCore 0:
  13.9 104.6 all-gather.5
  120.2 55.7 all-gather.3
  185.9 57.7 all-gather.7
where the time goes:
time: 260 us
  waiting for transfers between devices  218 us (84%)
  matrix products  19.4 us (7%)
  between operations  13.2 us (5%)
  local copies, waits for them, and re-layouts  5.25 us (2%)
    all_gather x1, waiting for transfers between devices, per_device(): col_panel = lax.all_gather(density, 'row', axis=0, tiled=True)  102 us
    all_gather x1, waiting for transfers between devices, per_device(): low_panel = lax.all_gather(square_low, 'col', axis=1, tiled=True)  58 us
    all_gather x1, waiting for transfers between devices, per_device(): row_panel = lax.all_gather(density, 'col', axis=1, tiled=True)  57.4 us
    dot_general x1, matrix products, per_device(): cubic = jnp.dot(low_panel, col_panel, preferred_element_type=jnp.float32)  9.75 us
    dot_general x1, matrix products, per_device(): jnp.dot(row_panel, col_panel, preferred_element_type=jnp.float32)  9.69 us
  transfers between devices with their start and end apart: 5, of which 3 were waited for; matrix products, arithmetic and copies ran while one was open for 2% of the time, Pallas kernels for 0%

commit v1 on v0

--- a/solution.py
+++ b/solution.py
@@ -3,11 +3,18 @@
 import jax.numpy as jnp
 from jax import lax
 from jax.sharding import PartitionSpec as P
+from jax.lax import all_to_all, axis_size
 
 BLK = 64
 BOX = 16
 NEAR = 40
 FAR = 90
+number_groups = lambda m, row_axis, axis_k: jnp.concatenate(
+    all_to_all(
+        jnp.stack([m] * axis_size(row_axis)), concat_axis=0, axis_name=row_axis, split_axis=0
+    ),
+    axis=axis_k,
+)
 
 
 def cell_mask(block_cells, row_start, row_count, col_start, col_count, bound_sq):
@@ -76,7 +83,7 @@
     col_panel = lax.all_gather(density, "row", axis=0, tiled=True)
     square = block_keep(jnp.dot(row_panel, col_panel, preferred_element_type=jnp.float32), far_own)
     square_low = square.astype(jnp.bfloat16)
-    low_panel = lax.all_gather(square_low, "col", axis=1, tiled=True)
+    low_panel = number_groups(square_low, "col", 1)
     cubic = jnp.dot(low_panel, col_panel, preferred_element_type=jnp.float32)
     return block_keep(3.0 * square - 2.0 * cubic, near_own).astype(jnp.bfloat16)
 

time: 260 us -> 311 us (1.20)
  blocking collectives: 0 us -> 110 us
  waiting for transfers between devices: 218 us -> 160 us
    all_to_all x0 -> x1, blocking collectives: none -> 110 us  [all_to_all(jnp.stack([m] * axis_size(row_axis)), concat_axis=0, axis_name...]
    all_gather x1 -> x0, waiting for transfers between devices: 58 us -> none  [per_device(): low_panel = lax.all_gather(square_low, 'col', axis=1, tiled=True)]
  transfers between devices with their start and end apart: 5 -> 4, of which waited for: 3 -> 2; matrix products, arithmetic and copies ran while one was open for 2% -> 1% of each run, Pallas kernels for 0% -> 0%
where the time goes in v1:
time: 311 us
  waiting for transfers between devices  160 us (51%)
  blocking collectives  110 us (35%)
  matrix products  17.3 us (6%)
  between operations  13.5 us (4%)
  local copies, waits for them, and re-layouts  6.41 us (2%)
    all_to_all x1, blocking collectives, all_to_all(jnp.stack([m] * axis_size(row_axis)), concat_axis=0, axis_name...  110 us
    all_gather x1, waiting for transfers between devices, per_device(): col_panel = lax.all_gather(density, 'row', axis=0, tiled=True)  102 us
    all_gather x1, waiting for transfers between devices, per_device(): row_panel = lax.all_gather(density, 'col', axis=1, tiled=True)  57.4 us
    dot_general x1, matrix products, per_device(): jnp.dot(row_panel, col_panel, preferred_element_type=jnp.float32)  8.99 us
    dot_general x1, matrix products, per_device(): cubic = jnp.dot(low_panel, col_panel, preferred_element_type=jnp.float32)  8.26 us
  transfers between devices with their start and end apart: 4, of which 2 were waited for; matrix products, arithmetic and copies ran while one was open for 1% of the time, Pallas kernels for 0%

profile of v1, /device:TPU:1, one launch (start us, length us, event | category | flops | bytes accessed | tf_op | source)
XLA Modules:
  0.0 311.2 jit_solution(3293001950741108667)
XLA Ops:
  6.5 0.0 copy-start
  6.5 0.0 all-gather.5.cloned.1.call-start
  6.5 1.1 constant_dynamic-slice_fusion.1
  7.7 0.2 copy.18
  7.9 1.5 collective-permute-start.1
  9.3 0.2 copy.17
  9.6 0.7 collective-permute-start
  10.3 0.0 copy-done
  10.3 0.1 constant_dynamic-slice_fusion.2
  10.3 0.1 constant_dynamic-slice_fusion.3
  10.4 0.1 fusion.4
  10.5 0.1 copy.12
  10.6 0.3 broadcast_in_dim.35
  10.9 0.0 copy-start.1
  10.9 1.4 broadcast_in_dim.36
  12.3 0.0 collective-permute-done.1
  12.3 0.0 collective-permute-done
  12.4 0.1 broadcast_select_fusion.1
  12.4 1.3 select_convert_fusion
  13.8 0.0 all-gather.5.cloned.1.call-update
  13.8 0.0 all-gather.3.cloned.1.call-start
  13.9 0.7 all-gather.3.cloned.1.call-update
  14.6 0.1 copy.13
  14.7 0.3 broadcast_in_dim.37
  14.9 1.4 broadcast_in_dim.38
  16.3 102.2 %all-gather.5.cloned.1.call-done = bf16[6144,384]{1,0:T(8,128)(2,1)} async-done(((bf16[768,384]{1,0:T(8,128)(2,1)}), bf16[6144,384]{1,0:T(8,128)(2,1)}) %all-gather.5.cloned.1.call-update) | async-done | bytes 4718608 | tf_op jit(solution)/shard_map/all_gather | solution.py:83
  118.6 57.4 %all-gather.3.cloned.1.call-done = bf16[768,6144]{1,0:T(8,128)(2,1)} async-done(((bf16[768,384]{1,0:T(8,128)(2,1)}), bf16[768,6144]{1,0:T(8,128)(2,1)}) %all-gather.3.cloned.1.call-update) | async-done | bytes 9437200 | tf_op jit(solution)/shard_map/all_gather | solution.py:82
  176.0 9.0 %fusion.5 = (bf16[768,384]{1,0:T(8,128)(2,1)S(1)}, f32[768,384]{1,0:T(8,128)S(1)}) fusion(pred[768,384]{1,0:T(32,128)(4,1)S(1)} %broadcast_in_dim.38, bf16[768,6144]{1,0:T(8,128)(2,1)} %all-gather.3.cloned.1.call-done, bf16[6144,384]{1,0:T(8,128)(2,1)} %all-gather.5.cloned.1.call-done), kind=kOutput, calls=%fused_computation.21 | convolution fusion | flops 3624468480 | bytes 16220160 | tf_op jit(solution)/shard_map/dot_general | solution.py:84
  185.0 0.3 copy.16
  185.3 0.9 stack.2
  186.2 109.9 %all_to_all.5 = bf16[16,768,384]{1,2,0:T(8,128)(2,1)S(1)} all-to-all(bf16[16,768,384]{1,2,0:T(8,128)(2,1)S(1)} %stack.2), channel_id=1, replica_groups=mesh['row'=8,'col'=16] {'col'}, dimensions={0} | all-to-all | bytes 18874368 | tf_op jit(solution)/shard_map/all_to_all | solution.py:13
  296.1 8.3 %fusion.2 = bf16[768,384]{1,0:T(8,128)(2,1)} fusion(pred[768,384]{1,0:T(32,128)(4,1)S(1)} %broadcast_in_dim.36, bf16[768,6144]{0,1:T(8,128)(2,1)S(1)} %bitcast.11, bf16[6144,384]{1,0:T(8,128)(2,1)} %all-gather.5.cloned.1.call-done, f32[768,384]{1,0:T(8,128)S(1)} %get-tuple-element.12), kind=kOutput, calls=%fused_computation.4 | convolution fusion | flops 3625353216 | bytes 16220160 | tf_op jit(solution)/shard_map/dot_general | solution.py:87
  (4 shorter events, 0.0 us)
Async XLA Ops:
  6.5 3.7 %copy-start = (s32[96,3]{0,1:T(4,128)S(1)}, s32[96,3]{0,1:T(4,128)}, u32[]{:S(2)}) copy-start(s32[96,3]{0,1:T(4,128)} %param.3) | copy-start | bytes 3460
  6.5 112.0 %all-gather.5.cloned.1.call-start = ((), (), s32[]{:S(2)}) async-start(), calls=%async_computation.2 | async-start | bytes 5308416 | tf_op jit(solution)/shard_map/all_gather | solution.py:83
  7.9 4.5 %collective-permute-start.1 = (bf16[384,384]{0,1:T(8,128)(2,1)S(1)}, bf16[384,384]{0,1:T(8,128)(2,1)S(1)}, u32[]{:S(2)}, u32[]{:S(2)}) collective-permute-start(bf16[384,384]{0,1:T(8,128)(2,1)S(1)} %copy.18), channel_id=1, source_target_pairs={{0,1},{1,0},{2,17},{3,16},{4,33},{5,32},{6,49},{7,48},{8,65},{9,64... | collective-permute-start | bytes 884744 | tf_op jit(solution)/shard_map/ppermute | solution.py:51
  9.6 2.8 collective-permute-start
  10.9 1.5 copy-start.1
  13.8 162.2 %all-gather.3.cloned.1.call-start = ((), (), s32[]{:S(2)}) async-start(), calls=%async_computation.1 | async-start | bytes 10027008 | tf_op jit(solution)/shard_map/all_gather | solution.py:82
Sparse Core Ops, SparseCore 0:
  13.9 104.6 all-gather.4
  120.2 55.7 all-gather.2
